TPU v7x, 128 devices: a whole 4x4x4 slice. The times are simulated.
128 devices in a mesh: grp: 32 (over z, y, core), head: 4 (over x).
Axes of the slice: x: 4, y: 4, z: 4, core: 2. Of those that a mesh axis runs over, the one named last changes fastest.
Arguments:
- activations: bfloat16 [1024, 4096], P('grp', 'head'), may hold values from -1.5 to 1.5
- ln_gain: bfloat16 [4096], replicated, may hold values from 0.099609375 to 1.8984375
- ln_bias: bfloat16 [4096], replicated, may hold values from -3 to 3
- w_qkv: bfloat16 [4096, 3, 4096], P('grp', None, 'head'), may hold values from -0.09375 to 0.09375
- prefix_keys: bfloat16 [64, 1024, 4096], P('grp', None, 'head')
- prefix_values: bfloat16 [64, 1024, 4096], P('grp', None, 'head'), may hold values from -6 to 6
- own_keys: bfloat16 [1024, 32, 4096], P('grp', None, 'head'), may hold values from -6 to 6
- own_values: bfloat16 [1024, 32, 4096], P('grp', None, 'head'), may hold values from -6 to 6
- prompt_len: int32 [64], P('grp'), may hold values from 64 to 1024, as said below
- own_len: int32 [1024], P('grp'), may hold values from 1 to 32, as said below
- w_attn_out: bfloat16 [256, 16, 4096], P('grp', 'head'), may hold values from -0.09375 to 0.09375
- w_in: bfloat16 [4096, 16384], P(None, ('grp', 'head')), may hold values from -0.09375 to 0.09375
- b_in: bfloat16 [16384], P(('grp', 'head')), may hold values from -4 to 4
- w_down: bfloat16 [16384, 4096], P(('grp', 'head')), may hold values from -0.046875 to 0.046875
- b_down: bfloat16 [4096], P('head'), may hold values from -3 to 3
Outputs:
- layer_out: bfloat16 [1024, 4096], P('grp', 'head')
Inputs may be any that keep to these rules, and one draw needn't show every extreme that they name: `prompt_len`: some group's prompt has exactly 1024 tokens and some has 64. `own_len`: some request has exactly 32 own tokens.
All inputs are finite; a program needn't handle non-finite values.
Results may differ from a plain program's by a relative error of at most 0.034.
Values may be sent and summed in bfloat16 or wider, within the bound.
No kernel may reach another device: no remote copies, remote signals or barrier semaphores. Data moves between devices by JAX's collectives and lax.ppermute only.
A program may use at most 128 MiB of HBM per device.

v0:
```python
import math
import jax
import jax.numpy as jnp
from jax import lax
from jax.sharding import PartitionSpec as P

HS = 256
ROT = 64
GSIZE = 16


def normalize(rows, gain, shift):
    floats = rows.astype(jnp.float32)
    center = floats - jnp.mean(floats, axis=-1, keepdims=True)
    spread = jnp.mean(center * center, axis=-1, keepdims=True)
    return (
        center * lax.rsqrt(spread + 1e-05) * gain.astype(jnp.float32) + shift.astype(jnp.float32)
    ).astype(jnp.bfloat16)


def rotate(values, positions):
    half = ROT // 2
    index = jnp.arange(half, dtype=jnp.float32)
    freqs = jnp.power(jnp.float32(10000.0), -2.0 * index / ROT)
    angle = positions[:, None, None] * freqs[None, None, :]
    cosine = jnp.cos(angle)
    sine = jnp.sin(angle)
    pairs = values[..., :ROT].reshape(values.shape[:-1] + (half, 2))
    first = pairs[..., 0]
    second = pairs[..., 1]
    turned = jnp.stack([first * cosine - second * sine, second * cosine + first * sine], axis=-1)
    turned = turned.reshape(values.shape[:-1] + (ROT,))
    return jnp.concatenate([turned, values[..., ROT:]], axis=-1)


def head_exchange(pieces, axis):
    count = lax.axis_size("head")
    here = lax.axis_index("head")
    received = []
    for shift in range(count):
        piece = lax.dynamic_index_in_dim(pieces, (here + shift) % count, axis, keepdims=False)
        if shift:
            piece = lax.ppermute(piece, "head", [(i, (i + shift) % count) for i in range(count)])
        received.append(piece)
    stacked = jnp.stack(received, axis=0)
    return jnp.take(stacked, (here - jnp.arange(count)) % count, axis=0)


def head_gather(piece):
    count = lax.axis_size("head")
    here = lax.axis_index("head")
    received = [piece]
    for shift in range(1, count):
        received.append(
            lax.ppermute(piece, "head", [(i, (i + shift) % count) for i in range(count)])
        )
    stacked = jnp.stack(received, axis=0)
    return jnp.take(stacked, (here - jnp.arange(count)) % count, axis=0)


def local(
    activations,
    ln_gain,
    ln_bias,
    w_qkv,
    prefix_keys,
    prefix_values,
    own_keys,
    own_values,
    prompt_len,
    own_len,
    w_attn_out,
    w_in,
    b_in,
    w_down,
    b_down,
):
    grp_count = lax.axis_size("grp")
    head_count = lax.axis_size("head")
    width_here = activations.shape[1]
    full_rows = jnp.moveaxis(head_gather(activations), 0, 1).reshape(activations.shape[0], -1)
    normed = normalize(full_rows, ln_gain, ln_bias)
    local_rows = normed.shape[0]
    groups_here = prompt_len.shape[0]
    gathered = lax.all_gather(normed, "grp", axis=0, tiled=True)
    block = w_qkv.shape[0]
    pair_rows = normed.reshape(local_rows, grp_count // 2, 2 * block)
    columns = lax.all_to_all(
        jnp.repeat(pair_rows, 2, axis=1), "grp", split_axis=1, concat_axis=0, tiled=True
    ).reshape(grp_count * local_rows, 2 * block)
    parity = lax.axis_index("grp") % 2
    half = w_qkv.shape[2] // 2
    own = lax.dynamic_slice_in_dim(w_qkv, parity * half, half, axis=2)
    other = lax.dynamic_slice_in_dim(w_qkv, (1 - parity) * half, half, axis=2)
    sibling = lax.ppermute(other, "grp", [(i, i ^ 1) for i in range(grp_count)])
    pair_weights = jnp.where(
        parity == 0,
        jnp.concatenate([own, sibling], axis=0),
        jnp.concatenate([sibling, own], axis=0),
    )
    term = jnp.einsum(
        "rf,fch->rch", columns, pair_weights, preferred_element_type=jnp.float32
    ).astype(jnp.bfloat16)
    received = lax.all_to_all(
        term.reshape(grp_count, local_rows, 3, half), "grp", 0, 0, tiled=True
    ).reshape(grp_count // 2, 2, local_rows, 3, half)
    qkv = jnp.sum(received.astype(jnp.float32), axis=0)
    qkv = jnp.transpose(qkv, (1, 2, 0, 3)).reshape(local_rows, 3, 2 * half)
    heads_here = w_qkv.shape[2] // HS
    member = (jnp.arange(local_rows) // GSIZE)[:, None] == jnp.arange(groups_here)[None, :]
    row_prompt = jnp.sum(jnp.where(member, prompt_len[None, :], 0), axis=1)
    positions = (row_prompt + own_len).astype(jnp.float32)
    query = rotate(qkv[:, 0].reshape(local_rows, heads_here, HS), positions).astype(jnp.bfloat16)
    key_new = rotate(qkv[:, 1].reshape(local_rows, heads_here, HS), positions).astype(jnp.bfloat16)
    value_new = qkv[:, 2].reshape(local_rows, heads_here, HS).astype(jnp.bfloat16)
    scale = 1.0 / math.sqrt(HS)
    longest = prefix_keys.shape[1]
    own_count = own_keys.shape[1]
    grouped = query.reshape(groups_here, GSIZE, heads_here, HS)
    pre_keys = prefix_keys.reshape(groups_here, longest, heads_here, HS)
    pre_vals = prefix_values.reshape(groups_here, longest, heads_here, HS)
    mine_keys = own_keys.reshape(local_rows, own_count, heads_here, HS)
    mine_vals = own_values.reshape(local_rows, own_count, heads_here, HS)
    pre_scores = (
        jnp.einsum("gqhd,gjhd->gqhj", grouped, pre_keys, preferred_element_type=jnp.float32) * scale
    )
    pre_scores = jnp.where(
        jnp.arange(longest)[None, None, None, :] < prompt_len[:, None, None, None],
        pre_scores,
        -jnp.inf,
    )
    own_scores = (
        jnp.einsum("rhd,rthd->rht", query, mine_keys, preferred_element_type=jnp.float32) * scale
    )
    own_scores = jnp.where(
        jnp.arange(own_count)[None, None, :] < own_len[:, None, None], own_scores, -jnp.inf
    )
    self_scores = (
        jnp.einsum("rhd,rhd->rh", query, key_new, preferred_element_type=jnp.float32) * scale
    )
    pre_peak = jnp.max(pre_scores, axis=-1).reshape(local_rows, heads_here)
    peak = jnp.maximum(jnp.maximum(pre_peak, jnp.max(own_scores, axis=-1)), self_scores)
    pre_exp = jnp.exp(pre_scores - peak.reshape(groups_here, GSIZE, heads_here)[..., None])
    own_exp = jnp.exp(own_scores - peak[..., None])
    self_exp = jnp.exp(self_scores - peak)
    denom = (
        jnp.sum(pre_exp, axis=-1).reshape(local_rows, heads_here)
        + jnp.sum(own_exp, axis=-1)
        + self_exp
    )
    mixed = jnp.einsum(
        "gqhj,gjhd->gqhd",
        pre_exp.astype(jnp.bfloat16),
        pre_vals,
        preferred_element_type=jnp.float32,
    )
    mixed = mixed.reshape(local_rows, heads_here, HS)
    mixed = mixed + jnp.einsum(
        "rht,rthd->rhd", own_exp.astype(jnp.bfloat16), mine_vals, preferred_element_type=jnp.float32
    )
    mixed = mixed + self_exp.astype(jnp.bfloat16).astype(jnp.float32)[..., None] * value_new.astype(
        jnp.float32
    )
    attended = (mixed / denom[..., None]).astype(jnp.bfloat16)
    dim_here = HS // grp_count
    outgoing = jnp.broadcast_to(
        jnp.transpose(attended.reshape(local_rows, heads_here, grp_count, dim_here), (2, 0, 1, 3))[
            :, None
        ],
        (grp_count, head_count, local_rows, heads_here, dim_here),
    ).reshape(grp_count * head_count, local_rows, heads_here, dim_here)
    incoming = lax.all_to_all(outgoing, ("grp", "head"), 0, 0, tiled=True).reshape(
        grp_count, head_count, local_rows, heads_here, dim_here
    )
    slices = jnp.transpose(incoming, (4, 1, 3, 0, 2)).reshape(
        dim_here, head_count * heads_here, grp_count * local_rows
    )
    out_blocks = head_exchange(w_attn_out.reshape(dim_here, heads_here, head_count, width_here), 2)
    out_blocks = jnp.moveaxis(out_blocks, 0, 1).reshape(
        dim_here, heads_here * head_count, width_here
    )
    units = w_in.shape[1]
    down_blocks = head_exchange(w_down.reshape(units, head_count, width_here), 1).reshape(
        units * head_count, width_here
    )
    hidden = jax.nn.gelu(
        jnp.dot(gathered, w_in, preferred_element_type=jnp.float32) + b_in.astype(jnp.float32),
        approximate=True,
    ).astype(jnp.bfloat16)
    hidden = lax.all_gather(hidden, "head", axis=1, tiled=True)
    mlp_part = jnp.dot(hidden, down_blocks, preferred_element_type=jnp.float32)
    attn_part = jnp.einsum("dkr,dkf->rf", slices, out_blocks, preferred_element_type=jnp.float32)
    combined = mlp_part + attn_part
    half_width = width_here // 2
    mine = lax.dynamic_slice_in_dim(combined, parity * half_width, half_width, axis=1)
    theirs = lax.dynamic_slice_in_dim(combined, (1 - parity) * half_width, half_width, axis=1)
    got = lax.ppermute(theirs.astype(jnp.bfloat16), "grp", [(i, i ^ 1) for i in range(grp_count)])
    pair_sum = (mine + got.astype(jnp.float32)).astype(jnp.bfloat16)
    pieces = lax.all_to_all(
        pair_sum.reshape(grp_count, local_rows, half_width), "grp", 0, 0, tiled=True
    ).reshape(grp_count // 2, 2, local_rows, half_width)
    summed = jnp.sum(pieces.astype(jnp.float32), axis=0)
    summed = jnp.transpose(summed, (1, 0, 2)).reshape(local_rows, width_here)
    total = activations.astype(jnp.float32) + b_down.astype(jnp.float32)[None, :] + summed
    return total.astype(jnp.bfloat16)


def solution(mesh):
    in_specs = (
        P("grp", "head"),
        P(),
        P(),
        P("grp", None, "head"),
        P("grp", None, "head"),
        P("grp", None, "head"),
        P("grp", None, "head"),
        P("grp", None, "head"),
        P("grp"),
        P("grp"),
        P("grp", "head", None),
        P(None, ("grp", "head")),
        P(("grp", "head")),
        P(("grp", "head"), None),
        P("head"),
    )
    out_specs = P("grp", "head")
    return jax.shard_map(local, mesh=mesh, in_specs=in_specs, out_specs=out_specs, check_vma=False)
```

profile of v0, /device:TPU:1, one launch (start us, length us, event | category | flops | bytes accessed | tf_op | source)
XLA Modules:
  0.0 190.7 jit_solution(12100319529735048736)
XLA Ops:
  6.5 2.1 %collective-permute-start = (bf16[32,1024]{1,0:T(8,128)(2,1)}, bf16[32,1024]{1,0:T(8,128)(2,1)S(1)}, u32[]{:S(2)}, u32[]{:S(2)}) collective-permute-start(bf16[32,1024]{1,0:T(8,128)(2,1)} %param.15), channel_id=1, source_target_pairs={{0,1},{1,2},{2,3},{3,0},{4,5},{5,6},{6,7},{7,4},{8,9},{9,10},{10,1... | collective-permute-start | bytes 196616 | tf_op jit(solution)/shard_map/ppermute | solution.py:55
  8.6 1.4 collective-permute-start.2
  10.0 1.6 collective-permute-start.1
  11.7 0.7 convert_element_type.107
  12.4 0.7 convert_element_type.108
  13.1 1.7 collective-permute-done.1
  14.8 0.9 pad_maximum_fusion.1
  17.0 0.9 add_convert_fusion.2
  18.9 0.9 broadcast_in_dim.106
  19.8 10.6 %all-to-all-start = ((bf16[32,32,256]{2,0,1:T(8,128)(2,1)}), bf16[32,32,256]{2,0,1:T(8,128)(2,1)S(1)}, u32[]{:S(2)}, u32[]{:S(2)}) async-start(bf16[32,32,256]{2,0,1:T(8,128)(2,1)} %bitcast.16), calls=%async_computation | async-start | bytes 1048576 | tf_op jit(solution)/shard_map/all_to_all | solution.py:88
  30.8 1.5 collective-permute-done.6
  32.3 12.1 %all-to-all-done = bf16[32,32,256]{2,0,1:T(8,128)(2,1)S(1)} async-done(((bf16[32,32,256]{2,0,1:T(8,128)(2,1)}), bf16[32,32,256]{2,0,1:T(8,128)(2,1)S(1)}, u32[]{:S(2)}, u32[]{:S(2)}) %all-to-all-start) | async-done | bytes 524320 | tf_op jit(solution)/shard_map/all_to_all | solution.py:88
  44.5 1.0 convolution_convert_fusion
  45.5 2.1 %copy.140 = bf16[32,32,3,512]{3,1,2,0:T(8,128)(2,1)} copy(bf16[32,32,3,512]{3,1,0,2:T(8,128)(2,1)S(1)} %bitcast.166) | data formatting | bytes 6291456 | tf_op jit(solution)/shard_map/reshape | solution.py:105
  47.6 4.9 %all-to-all-start.1 = ((bf16[32,32,3,512]{3,1,2,0:T(8,128)(2,1)}), bf16[32,32,3,512]{3,1,2,0:T(8,128)(2,1)}, u32[]{:S(2)}, u32[]{:S(2)}) async-start(bf16[32,32,3,512]{3,1,2,0:T(8,128)(2,1)} %copy.140), calls=%async_computation.1 | async-start | bytes 6291456 | tf_op jit(solution)/shard_map/all_to_all | solution.py:104
  53.6 0.7 copy.261
  54.3 0.9 collective-permute-start.9
  55.2 0.7 copy.263
  57.2 1.2 collective-permute-start.8
  59.2 1.6 collective-permute-start.3
  61.0 1.0 collective-permute-start.4
  63.4 0.7 multiply_cosine_fusion
  64.1 1.2 broadcast_bitcast_fusion
  65.3 1.2 convert_element_type.110
  66.9 1.8 collective-permute-start.5
  68.6 0.9 pad_maximum_fusion.2
  70.3 1.4 broadcast_select_fusion
  71.7 2.6 %collective-permute-done.4 = bf16[128,1024]{1,0:T(8,128)(2,1)} collective-permute-done((bf16[128,1024]{1,0:T(8,128)(2,1)S(1)}, bf16[128,1024]{1,0:T(8,128)(2,1)}, u32[]{:S(2)}, u32[]{:S(2)}) %collective-permute-start.4) | collective-permute-done | bytes 262176 | tf_op jit(solution)/shard_map/ppermute | solution.py:43
  74.3 0.7 copy-done.7
  75.0 1.2 pad_maximum_fusion
  76.2 0.7 gather_fusion.1
  76.9 32.3 %all-to-all-done.1 = bf16[32,32,3,512]{3,1,2,0:T(8,128)(2,1)} async-done(((bf16[32,32,3,512]{3,1,2,0:T(8,128)(2,1)}), bf16[32,32,3,512]{3,1,2,0:T(8,128)(2,1)}, u32[]{:S(2)}, u32[]{:S(2)}) %all-to-all-start.1) | async-done | bytes 3145760 | tf_op jit(solution)/shard_map/all_to_all | solution.py:104
  109.3 2.5 %convert_reduce_fusion = f32[2,32,3,512]{3,1,2,0:T(8,128)S(1)} fusion(bf16[16,2,32,3,512]{4,2,3,1,0:T(8,128)(2,1)} %bitcast.53), kind=kLoop, calls=%fused_computation.3 | loop fusion | flops 3047424 | bytes 3538944 | tf_op jit(solution)/shard_map/reduce_sum | solution.py:107
  114.2 3.5 %fusion.68 = (f32[2,16,4]{1,2,0:T(4,128)S(1)}, f32[2,16,4,1024]{3,1,2,0:T(8,128)S(1)}) fusion(bf16[2,128,4,8,256]{4,3,2,1,0:T(8,128)(2,1)} %bitcast.161, bf16[2,16,4,64]{3,1,2,0:T(8,128)(2,1)S(1)} %copy.145, pred[2,1024]{1,0:T(4,128)(4,1)S(1)} %copy-done.12, bf16[2,16,4,192]{3,1,0,2:T(8,128)(2,1)S(1)} %bitcast.173), kind=kOutput, calls=%fused_computation.142 | convolution fusion | flops 67633024 | bytes 4786688 | tf_op jit(solution)/shard_map/gqhd,gjhd->gqhj/dot_general | solution.py:125
  117.7 2.2 %fusion.9 = f32[32,4,1,32]{3,2,1,0:T(1,128)S(1)} fusion(bf16[32,4,4,8,256]{4,3,2,1,0:T(8,128)(2,1)} %bitcast.192, bf16[32,4,256,1]{2,0,1,3:T(8,128)(2,1)S(1)} %get-tuple-element.25), kind=kOutput, calls=%fused_computation.15 | convolution fusion | flops 2097152 | bytes 2179072 | tf_op jit(solution)/shard_map/rhd,rthd->rht/dot_general | solution.py:133
  120.2 6.5 %fusion.37 = bf16[1024,128]{1,0:T(8,128)(2,1)} fusion(bf16[1024,4096]{1,0:T(8,128)(2,1)} %all-gather.3.cloned.1.call-done, bf16[4096,128]{1,0:T(8,128)(2,1)S(1)} %copy-done, f32[128]{0:T(128)S(1)} %copy-done.19), kind=kOutput, calls=%fused_computation.47 | convolution fusion | flops 1075052544 | bytes 9699840 | tf_op jit(solution)/shard_map/dot_general | solution.py:187
  126.7 2.9 %fusion.21 = f32[2,16,4,256]{3,1,2,0:T(8,128)S(1)} fusion(bf16[2,128,4,8,256]{4,3,2,1,0:T(8,128)(2,1)} %bitcast.164, f32[2,16,4,1024]{3,1,2,0:T(8,128)S(1)} %get-tuple-element.32, f32[2,16,4]{1,2,0:T(4,128)S(1)} %copy.152), kind=kOutput, calls=%fused_computation.25 | convolution fusion | flops 67371008 | bytes 4850176 | tf_op jit(solution)/shard_map/gqhj,gjhd->gqhd/dot_general | solution.py:151
  130.1 2.0 %fusion.6 = f32[32,4,1,256]{3,2,1,0:T(1,128)S(1)} fusion(bf16[32,4,4,8,256]{4,3,2,1,0:T(8,128)(2,1)} %bitcast.193, bf16[32,4,32,1]{2,0,1,3:T(8,128)(2,1)S(1)} %get-tuple-element.28), kind=kOutput, calls=%fused_computation.12 | convolution fusion | flops 2097152 | bytes 2236416 | tf_op jit(solution)/shard_map/rht,rthd->rhd/dot_general | solution.py:158
  132.7 1.5 reshape.381
  134.2 4.1 %all-to-all-start.2 = ((bf16[128,2,512]{2,1,0:T(2,128)(2,1)}), bf16[128,2,512]{2,1,0:T(2,128)(2,1)S(1)}, u32[]{:S(2)}, u32[]{:S(2)}) async-start(bf16[128,2,512]{2,1,0:T(2,128)(2,1)} %reshape.381), calls=%async_computation.2 | async-start | bytes 524288 | tf_op jit(solution)/shard_map/all_to_all | solution.py:172
  138.5 12.8 %all-to-all-done.2 = bf16[128,2,512]{2,1,0:T(2,128)(2,1)S(1)} async-done(((bf16[128,2,512]{2,1,0:T(2,128)(2,1)}), bf16[128,2,512]{2,1,0:T(2,128)(2,1)S(1)}, u32[]{:S(2)}, u32[]{:S(2)}) %all-to-all-start.2) | async-done | bytes 262176 | tf_op jit(solution)/shard_map/all_to_all | solution.py:172
  152.5 1.1 reshape.334
  153.6 2.5 %fusion.69 = f32[1024,1024]{1,0:T(8,128)S(1)} fusion(bf16[1024,512]{1,0:T(8,128)(2,1)} %all-gather.5.cloned.1.call-done, bf16[512,1024]{1,0:T(8,128)(2,1)S(1)} %bitcast_select_fusion), kind=kOutput, calls=%fused_computation.143 | convolution fusion | flops 1073741824 | bytes 6291456 | tf_op jit(solution)/shard_map/dot_general | solution.py:191
  156.1 0.8 bitcast_add_fusion
  157.6 2.3 %collective-permute-done.10 = bf16[1024,512]{1,0:T(8,128)(2,1)S(1)} collective-permute-done((bf16[1024,512]{1,0:T(8,128)(2,1)S(1)}, bf16[1024,512]{1,0:T(8,128)(2,1)S(1)}, u32[]{:S(2)}, u32[]{:S(2)}) %collective-permute-start.10) | collective-permute-done | bytes 1048608 | tf_op jit(solution)/shard_map/ppermute | solution.py:197
  159.9 1.4 add_convert_fusion
  161.3 4.7 %all-to-all-start.3 = ((bf16[32,32,512]{2,1,0:T(8,128)(2,1)}), bf16[32,32,512]{2,1,0:T(8,128)(2,1)S(1)}, u32[]{:S(2)}, u32[]{:S(2)}) async-start(bf16[32,32,512]{2,1,0:T(8,128)(2,1)} %bitcast.47), calls=%async_computation.3 | async-start | bytes 2097152 | tf_op jit(solution)/shard_map/all_to_all | solution.py:199
  166.0 17.0 %all-to-all-done.3 = bf16[32,32,512]{2,1,0:T(8,128)(2,1)S(1)} async-done(((bf16[32,32,512]{2,1,0:T(8,128)(2,1)}), bf16[32,32,512]{2,1,0:T(8,128)(2,1)S(1)}, u32[]{:S(2)}, u32[]{:S(2)}) %all-to-all-start.3) | async-done | bytes 1048608 | tf_op jit(solution)/shard_map/all_to_all | solution.py:199
  (137 shorter events, 14.7 us)
Async XLA Ops:
  6.5 113.7 %copy-start = (bf16[4096,128]{1,0:T(8,128)(2,1)S(1)}, bf16[4096,128]{1,0:T(8,128)(2,1)}, u32[]{:S(2)}) copy-start(bf16[4096,128]{1,0:T(8,128)(2,1)} %param.26) | copy-start | bytes 3145732
  6.5 11.4 %copy-start.10 = (bf16[4096]{0:T(1024)(128)(2,1)S(1)}, bf16[4096]{0:T(1024)(128)(2,1)}, u32[]{:S(2)}) copy-start(bf16[4096]{0:T(1024)(128)(2,1)} %param.16) | copy-start | bytes 24580
  6.5 11.4 %copy-start.11 = (bf16[4096]{0:T(1024)(128)(2,1)S(1)}, bf16[4096]{0:T(1024)(128)(2,1)}, u32[]{:S(2)}) copy-start(bf16[4096]{0:T(1024)(128)(2,1)} %param.17) | copy-start | bytes 24580
  6.5 113.7 %all-gather.3.cloned.1.call-start = ((), (), s32[]{:S(2)}) async-start(), calls=%async_computation.4 | async-start | bytes 8650752 | tf_op jit(solution)/shard_map/all_gather | solution.py:85
  6.5 6.6 %collective-permute-start = (bf16[32,1024]{1,0:T(8,128)(2,1)}, bf16[32,1024]{1,0:T(8,128)(2,1)S(1)}, u32[]{:S(2)}, u32[]{:S(2)}) collective-permute-start(bf16[32,1024]{1,0:T(8,128)(2,1)} %param.15), channel_id=1, source_target_pairs={{0,1},{1,2},{2,3},{3,0},{4,5},{5,6},{6,7},{7,4},{8,9},{9,10},{10,1... | collective-permute-start | bytes 196616 | tf_op jit(solution)/shard_map/ppermute | solution.py:55
  8.6 4.5 %collective-permute-start.2 = (bf16[32,1024]{1,0:T(8,128)(2,1)}, bf16[32,1024]{1,0:T(8,128)(2,1)S(1)}, u32[]{:S(2)}, u32[]{:S(2)}) collective-permute-start(bf16[32,1024]{1,0:T(8,128)(2,1)} %param.15), channel_id=1, source_target_pairs={{0,3},{1,0},{2,1},{3,2},{4,7},{5,4},{6,5},{7,6},{8,11},{9,8},{10,9... | collective-permute-start | bytes 196616 | tf_op jit(solution)/shard_map/ppermute | solution.py:55
  10.0 4.8 %collective-permute-start.1 = (bf16[32,1024]{1,0:T(8,128)(2,1)}, bf16[32,1024]{1,0:T(8,128)(2,1)S(1)}, u32[]{:S(2)}, u32[]{:S(2)}) collective-permute-start(bf16[32,1024]{1,0:T(8,128)(2,1)} %param.15), channel_id=1, source_target_pairs={{0,2},{1,3},{2,0},{3,1},{4,6},{5,7},{6,4},{7,5},{8,10},{9,11},{10,... | collective-permute-start | bytes 196616 | tf_op jit(solution)/shard_map/ppermute | solution.py:55
  11.7 4.6 %copy-start.14 = (s32[1024]{0:T(1024)}, s32[1024]{0:T(1024)S(1)}, u32[]{:S(2)}) copy-start(s32[1024]{0:T(1024)S(1)} %pad_clamp_fusion) | copy-start | bytes 12292
  13.1 4.9 %copy-start.13 = (pred[4]{0:T(512)(128)(4,1)}, pred[4]{0:T(512)(128)(4,1)S(1)}, u32[]{:S(2)}) copy-start(pred[4]{0:T(512)(128)(4,1)S(1)} %compare_and_fusion) | copy-start | bytes 16
  17.0 13.4 %copy-start.3 = (bf16[128,3,1024]{2,0,1:T(8,128)(2,1)S(1)}, bf16[128,3,1024]{2,0,1:T(8,128)(2,1)}, u32[]{:S(2)}) copy-start(bf16[128,3,1024]{2,0,1:T(8,128)(2,1)} %param.18) | copy-start | bytes 2359300
  19.8 24.6 %all-to-all-start = ((bf16[32,32,256]{2,0,1:T(8,128)(2,1)}), bf16[32,32,256]{2,0,1:T(8,128)(2,1)S(1)}, u32[]{:S(2)}, u32[]{:S(2)}) async-start(bf16[32,32,256]{2,0,1:T(8,128)(2,1)} %bitcast.16), calls=%async_computation | async-start | bytes 1048576 | tf_op jit(solution)/shard_map/all_to_all | solution.py:88
  30.5 1.8 collective-permute-start.6
  47.6 5.0 %copy-start.5 = (bf16[8,4,4096]{2,1,0:T(4,128)(2,1)S(1)}, bf16[8,4,4096]{2,1,0:T(4,128)(2,1)}, u32[]{:S(2)}) copy-start(bf16[8,4,4096]{2,1,0:T(4,128)(2,1)} %param.25) | copy-start | bytes 786436
  47.6 10.7 %copy-start.2 = (bf16[128,4096]{1,0:T(8,128)(2,1)S(1)}, bf16[128,4096]{1,0:T(8,128)(2,1)}, u32[]{:S(2)}) copy-start(bf16[128,4096]{1,0:T(8,128)(2,1)} %param.28) | copy-start | bytes 3145732
  47.6 61.6 %all-to-all-start.1 = ((bf16[32,32,3,512]{3,1,2,0:T(8,128)(2,1)}), bf16[32,32,3,512]{3,1,2,0:T(8,128)(2,1)}, u32[]{:S(2)}, u32[]{:S(2)}) async-start(bf16[32,32,3,512]{3,1,2,0:T(8,128)(2,1)} %copy.140), calls=%async_computation.1 | async-start | bytes 6291456 | tf_op jit(solution)/shard_map/all_to_all | solution.py:104
  52.6 101.0 %all-gather.5.cloned.1.call-start = ((), (), s32[]{:S(2)}) async-start(), calls=%async_computation.5 | async-start | bytes 1310720 | tf_op jit(solution)/shard_map/all_gather | solution.py:190
  53.6 8.4 %copy-start.18 = (s32[2]{0:T(128)S(1)}, s32[2]{0:T(128)}, u32[]{:S(2)}) copy-start(s32[2]{0:T(128)} %param.23) | copy-start | bytes 28
  53.6 8.5 %copy-start.17 = (s32[32]{0:T(128)S(1)}, s32[32]{0:T(128)}, u32[]{:S(2)}) copy-start(s32[32]{0:T(128)} %param.24) | copy-start | bytes 388
  54.3 12.6 %collective-permute-start.9 = (bf16[8,4,1024]{2,0,1:T(8,128)(2,1)}, bf16[8,4,1024]{2,0,1:T(8,128)(2,1)}, u32[]{:S(2)}, u32[]{:S(2)}) collective-permute-start(bf16[8,4,1024]{2,0,1:T(8,128)(2,1)} %bitcast.156), channel_id=1, source_target_pairs={{0,3},{1,0},{2,1},{3,2},{4,7},{5,4},{6,5},{7,6},{8,11},{9,8},{10,9... | collective-permute-start | bytes 196616 | tf_op jit(solution)/shard_map/ppermute | solution.py:43
  55.9 12.8 %collective-permute-start.7 = (bf16[8,4,1024]{2,0,1:T(8,128)(2,1)}, bf16[8,4,1024]{2,0,1:T(8,128)(2,1)}, u32[]{:S(2)}, u32[]{:S(2)}) collective-permute-start(bf16[8,4,1024]{2,0,1:T(8,128)(2,1)} %bitcast.158), channel_id=1, source_target_pairs={{0,1},{1,2},{2,3},{3,0},{4,5},{5,6},{6,7},{7,4},{8,9},{9,10},{10,1... | collective-permute-start | bytes 196616 | tf_op jit(solution)/shard_map/ppermute | solution.py:43
  57.2 11.5 %collective-permute-start.8 = (bf16[8,4,1024]{2,0,1:T(8,128)(2,1)}, bf16[8,4,1024]{2,0,1:T(8,128)(2,1)}, u32[]{:S(2)}, u32[]{:S(2)}) collective-permute-start(bf16[8,4,1024]{2,0,1:T(8,128)(2,1)} %bitcast.157), channel_id=1, source_target_pairs={{0,2},{1,3},{2,0},{3,1},{4,6},{5,7},{6,4},{7,5},{8,10},{9,11},{10,... | collective-permute-start | bytes 196616 | tf_op jit(solution)/shard_map/ppermute | solution.py:43
  59.2 12.5 %collective-permute-start.3 = (bf16[128,1024]{1,0:T(8,128)(2,1)S(1)}, bf16[128,1024]{1,0:T(8,128)(2,1)S(1)}, u32[]{:S(2)}, u32[]{:S(2)}) collective-permute-start(bf16[128,1024]{1,0:T(8,128)(2,1)S(1)} %bitcast.182), channel_id=1, source_target_pairs={{0,1},{1,2},{2,3},{3,0},{4,5},{5,6},{6,7},{7,4},{8,9},{9,10},{10,1... | collective-permute-start | bytes 786440 | tf_op jit(solution)/shard_map/ppermute | solution.py:43
  61.0 13.3 %collective-permute-start.4 = (bf16[128,1024]{1,0:T(8,128)(2,1)S(1)}, bf16[128,1024]{1,0:T(8,128)(2,1)}, u32[]{:S(2)}, u32[]{:S(2)}) collective-permute-start(bf16[128,1024]{1,0:T(8,128)(2,1)S(1)} %bitcast.183), channel_id=1, source_target_pairs={{0,2},{1,3},{2,0},{3,1},{4,6},{5,7},{6,4},{7,5},{8,10},{9,11},{10,... | collective-permute-start | bytes 786440 | tf_op jit(solution)/shard_map/ppermute | solution.py:43
  66.9 7.4 %collective-permute-start.5 = (bf16[128,1024]{1,0:T(8,128)(2,1)S(1)}, bf16[128,1024]{1,0:T(8,128)(2,1)S(1)}, u32[]{:S(2)}, u32[]{:S(2)}) collective-permute-start(bf16[128,1024]{1,0:T(8,128)(2,1)S(1)} %bitcast.184), channel_id=1, source_target_pairs={{0,3},{1,0},{2,1},{3,2},{4,7},{5,4},{6,5},{7,6},{8,11},{9,8},{10,9... | collective-permute-start | bytes 786440 | tf_op jit(solution)/shard_map/ppermute | solution.py:43
  74.3 0.7 copy-start.7
  109.3 3.2 %copy-start.8 = (f32[32,32]{0,1:T(8,128)S(1)}, f32[32,32]{0,1:T(8,128)}, u32[]{:S(2)}) copy-start(f32[32,32]{0,1:T(8,128)} %get-tuple-element.30) | copy-start | bytes 12292
  111.8 2.4 %copy-start.12 = (pred[2,1024]{1,0:T(4,128)(4,1)S(1)}, pred[2,1024]{1,0:T(4,128)(4,1)}, u32[]{:S(2)}) copy-start(pred[2,1024]{1,0:T(4,128)(4,1)} %iota_compare_fusion.1) | copy-start | bytes 6148
  114.2 5.8 %copy-start.9 = (pred[32,32]{1,0:T(8,128)(4,1)S(1)}, pred[32,32]{1,0:T(8,128)(4,1)}, u32[]{:S(2)}) copy-start(pred[32,32]{1,0:T(8,128)(4,1)} %iota_compare_fusion) | copy-start | bytes 3076
  114.2 6.0 %copy-start.19 = (f32[128]{0:T(128)S(1)}, f32[128]{0:T(128)}, u32[]{:S(2)}) copy-start(f32[128]{0:T(128)} %convert_element_type.110) | copy-start | bytes 1540
  130.1 8.1 %copy-start.16 = (pred[512]{0:T(512)(128)(4,1)S(1)}, pred[512]{0:T(512)(128)(4,1)}, u32[]{:S(2)}) copy-start(pred[512]{0:T(512)(128)(4,1)} %broadcast_bitcast_fusion) | copy-start | bytes 1540
  134.2 17.1 %all-to-all-start.2 = ((bf16[128,2,512]{2,1,0:T(2,128)(2,1)}), bf16[128,2,512]{2,1,0:T(2,128)(2,1)S(1)}, u32[]{:S(2)}, u32[]{:S(2)}) async-start(bf16[128,2,512]{2,1,0:T(2,128)(2,1)} %reshape.381), calls=%async_computation.2 | async-start | bytes 524288 | tf_op jit(solution)/shard_map/all_to_all | solution.py:172
  153.6 2.6 %copy-start.4 = (bf16[4,8,4,1024]{3,1,2,0:T(8,128)(2,1)S(1)}, bf16[4,8,4,1024]{3,1,2,0:T(8,128)(2,1)}, u32[]{:S(2)}) copy-start(bf16[4,8,4,1024]{3,1,2,0:T(8,128)(2,1)} %broadcast_select_fusion) | copy-start | bytes 786436
  156.9 26.9 %copy-start.1 = (bf16[4096,128]{1,0:T(8,128)(2,1)S(1)}, bf16[4096,128]{1,0:T(8,128)(2,1)}, u32[]{:S(2)}) copy-start(bf16[4096,128]{1,0:T(8,128)(2,1)} %param.26) | copy-start | bytes 3145732
  157.1 8.9 %copy-start.15 = (bf16[1024]{0:T(1024)(128)(2,1)S(1)}, bf16[1024]{0:T(1024)(128)(2,1)}, u32[]{:S(2)}) copy-start(bf16[1024]{0:T(1024)(128)(2,1)} %param.29) | copy-start | bytes 6148
  157.1 26.1 %copy-start.6 = (bf16[32,1024]{1,0:T(8,128)(2,1)S(1)}, bf16[32,1024]{1,0:T(8,128)(2,1)}, u32[]{:S(2)}) copy-start(bf16[32,1024]{1,0:T(8,128)(2,1)} %param.15) | copy-start | bytes 196612
  157.1 2.8 %collective-permute-start.10 = (bf16[1024,512]{1,0:T(8,128)(2,1)S(1)}, bf16[1024,512]{1,0:T(8,128)(2,1)S(1)}, u32[]{:S(2)}, u32[]{:S(2)}) collective-permute-start(bf16[1024,512]{1,0:T(8,128)(2,1)S(1)} %dynamic-slice_convert_fusion), channel_id=1, source_target_pairs={{0,4},{4,0},{8,12},{12,8},{16,20},{20,16},{24,28},{28,24},{32,36},... | collective-permute-start | bytes 3145736 | tf_op jit(solution)/shard_map/ppermute | solution.py:197
  161.3 21.7 %all-to-all-start.3 = ((bf16[32,32,512]{2,1,0:T(8,128)(2,1)}), bf16[32,32,512]{2,1,0:T(8,128)(2,1)S(1)}, u32[]{:S(2)}, u32[]{:S(2)}) async-start(bf16[32,32,512]{2,1,0:T(8,128)(2,1)} %bitcast.47), calls=%async_computation.3 | async-start | bytes 2097152 | tf_op jit(solution)/shard_map/all_to_all | solution.py:199
Sparse Core Ops, SparseCore 0:
  18.0 90.7 all-gather.2
  126.8 22.8 all-gather.4
where the time goes:
time: 192 us; the launch traced here: 191 us
  waiting for transfers between devices  82.4 us (43%)
  starting transfers between devices  37.1 us (19%)
  matrix products  21.4 us (11%)
  local copies, waits for them, and re-layouts  18 us (9%)
  other arithmetic  17.4 us (9%)
  between operations  14.3 us (7%)
    all_to_all x1, waiting for transfers between devices, local(): lax.all_to_all(term.reshape(grp_count, local_rows, 3, half), 'grp', 0, 0,...  32.3 us
    all_to_all x1, waiting for transfers between devices, local(): lax.all_to_all(pair_sum.reshape(grp_count, local_rows, half_width), 'grp'...  17 us
    all_to_all x1, waiting for transfers between devices, local(): lax.all_to_all(outgoing, ('grp', 'head'), 0, 0, tiled=True)  12.8 us
    all_to_all x1, waiting for transfers between devices, local(): lax.all_to_all(jnp.repeat(pair_rows, 2, axis=1), 'grp', split_axis=1, con...  12.1 us
    all_to_all x1, starting transfers between devices, local(): lax.all_to_all(jnp.repeat(pair_rows, 2, axis=1), 'grp', split_axis=1, con...  10.6 us
    ppermute x6, starting transfers between devices, head_exchange(): lax.ppermute(piece, 'head', [(i, (i + shift) % count) for i in range(coun...  6.95 us
    dot_general x1, matrix products, local(): jnp.dot(gathered, w_in, preferred_element_type=jnp.float32)  6.47 us
    unnamed x50, local copies, waits for them, and re-layouts  5.88 us
  transfers between devices with their start and end apart: 17, of which 8 were waited for; matrix products, arithmetic and copies ran while one was open for 21% of the time, Pallas kernels for 0%

commit v1 on v0

--- a/solution.py
+++ b/solution.py
@@ -85,8 +85,14 @@
     gathered = lax.all_gather(normed, "grp", axis=0, tiled=True)
     block = w_qkv.shape[0]
     pair_rows = normed.reshape(local_rows, grp_count // 2, 2 * block)
-    columns = lax.all_to_all(
-        jnp.repeat(pair_rows, 2, axis=1), "grp", split_axis=1, concat_axis=0, tiled=True
+    columns = jnp.concatenate(
+        lax.all_to_all(
+            jnp.stack(jnp.split(jnp.repeat(pair_rows, 2, axis=1), lax.axis_size("grp"), axis=1)),
+            "grp",
+            0,
+            0,
+        ),
+        axis=0,
     ).reshape(grp_count * local_rows, 2 * block)
     parity = lax.axis_index("grp") % 2
     half = w_qkv.shape[2] // 2

time: 192 us -> 195 us (1.016)
  waiting for transfers between devices: 82.4 us -> 64.1 us
  local copies, waits for them, and re-layouts: 18 us -> 36.3 us
  starting transfers between devices: 37.1 us -> 40.2 us
    unnamed x50 -> x81, local copies, waits for them, and re-layouts: 5.88 us -> 24.5 us
    all_to_all x1, waiting for transfers between devices: 32.3 us -> 14.3 us  [local(): lax.all_to_all(term.reshape(grp_count, local_rows, 3, half), 'grp', 0, 0,...]
    all_to_all x1, starting transfers between devices: 4.06 us -> 7.16 us  [local(): lax.all_to_all(outgoing, ('grp', 'head'), 0, 0, tiled=True)]
  transfers between devices with their start and end apart: 17 -> 17, of which waited for: 8 -> 8; matrix products, arithmetic and copies ran while one was open for 21% -> 31% of each run, Pallas kernels for 0% -> 0%
where the time goes in v1:
time: 195 us; the launch traced here: 194 us
  waiting for transfers between devices  64.1 us (33%)
  starting transfers between devices  40.2 us (21%)
  local copies, waits for them, and re-layouts  36.3 us (19%)
  matrix products  21.4 us (11%)
  other arithmetic  17.4 us (9%)
  between operations  14.3 us (7%)
    unnamed x81, local copies, waits for them, and re-layouts  24.5 us
    all_to_all x1, waiting for transfers between devices, local(): lax.all_to_all(pair_sum.reshape(grp_count, local_rows, half_width), 'grp'...  17 us
    all_to_all x1, waiting for transfers between devices, local(): lax.all_to_all(term.reshape(grp_count, local_rows, 3, half), 'grp', 0, 0,...  14.3 us
    all_to_all x1, waiting for transfers between devices, local(): lax.all_to_all(outgoing, ('grp', 'head'), 0, 0, tiled=True)  12.9 us
    all_to_all x1, waiting for transfers between devices, local(): lax.all_to_all(jnp.stack(jnp.split(jnp.repeat(pair_rows, 2, axis=1), lax....  11.8 us
    all_to_all x1, starting transfers between devices, local(): lax.all_to_all(jnp.stack(jnp.split(jnp.repeat(pair_rows, 2, axis=1), lax....  10.6 us
    all_to_all x1, starting transfers between devices, local(): lax.all_to_all(outgoing, ('grp', 'head'), 0, 0, tiled=True)  7.16 us
    ppermute x6, starting transfers between devices, head_exchange(): lax.ppermute(piece, 'head', [(i, (i + shift) % count) for i in range(coun...  6.9 us
  transfers between devices with their start and end apart: 17, of which 8 were waited for; matrix products, arithmetic and copies ran while one was open for 31% of the time, Pallas kernels for 0%

profile of v1, /device:TPU:1, one launch (start us, length us, event | category | flops | bytes accessed | tf_op | source)
XLA Modules:
  0.0 193.7 jit_solution(17578902579738434299)
XLA Ops:
  6.5 2.1 %collective-permute-start = (bf16[32,1024]{1,0:T(8,128)(2,1)}, bf16[32,1024]{1,0:T(8,128)(2,1)S(1)}, u32[]{:S(2)}, u32[]{:S(2)}) collective-permute-start(bf16[32,1024]{1,0:T(8,128)(2,1)} %param.15), channel_id=1, source_target_pairs={{0,1},{1,2},{2,3},{3,0},{4,5},{5,6},{6,7},{7,4},{8,9},{9,10},{10,1... | collective-permute-start | bytes 196616 | tf_op jit(solution)/shard_map/ppermute | solution.py:55
  8.6 1.4 collective-permute-start.2
  10.0 1.6 collective-permute-start.1
  11.7 0.7 convert_element_type.107
  12.4 0.7 convert_element_type.108
  13.1 1.7 collective-permute-done.1
  14.8 0.9 pad_maximum_fusion.1
  17.0 0.9 add_convert_fusion.2
  38.2 10.6 %all-to-all-start = ((bf16[32,32,1,256]{3,1,2,0:T(8,128)(2,1)}), bf16[32,32,1,256]{3,1,2,0:T(8,128)(2,1)S(1)}, u32[]{:S(2)}, u32[]{:S(2)}) async-start(bf16[32,32,1,256]{3,1,2,0:T(8,128)(2,1)} %constant_dynamic-update-slice_fusion), calls=%async_computation | async-start | bytes 1048576 | tf_op jit(solution)/shard_map/all_to_all | solution.py:89
  49.2 1.5 collective-permute-done.6
  50.7 11.8 %all-to-all-done = bf16[32,32,1,256]{3,1,2,0:T(8,128)(2,1)S(1)} async-done(((bf16[32,32,1,256]{3,1,2,0:T(8,128)(2,1)}), bf16[32,32,1,256]{3,1,2,0:T(8,128)(2,1)S(1)}, u32[]{:S(2)}, u32[]{:S(2)}) %all-to-all-start) | async-done | bytes 524320 | tf_op jit(solution)/shard_map/all_to_all | solution.py:89
  62.5 1.0 convolution_convert_fusion
  63.5 2.1 %copy.233 = bf16[32,32,3,512]{3,1,2,0:T(8,128)(2,1)} copy(bf16[32,32,3,512]{3,1,0,2:T(8,128)(2,1)S(1)} %bitcast.290) | data formatting | bytes 6291456 | tf_op jit(solution)/shard_map/reshape | solution.py:111
  65.6 5.1 %all-to-all-start.1 = ((bf16[32,32,3,512]{3,1,2,0:T(8,128)(2,1)}), bf16[32,32,3,512]{3,1,2,0:T(8,128)(2,1)}, u32[]{:S(2)}, u32[]{:S(2)}) async-start(bf16[32,32,3,512]{3,1,2,0:T(8,128)(2,1)} %copy.233), calls=%async_computation.1 | async-start | bytes 6291456 | tf_op jit(solution)/shard_map/all_to_all | solution.py:110
  71.8 0.7 copy.354
  72.6 0.7 copy.356
  73.3 1.3 collective-permute-start.7
  74.7 0.7 copy.355
  76.6 1.6 collective-permute-start.3
  78.4 1.7 collective-permute-start.4
  81.6 0.7 multiply_cosine_fusion
  82.3 1.2 broadcast_bitcast_fusion
  83.5 1.2 convert_element_type.110
  85.1 1.7 collective-permute-start.5
  86.8 0.9 pad_maximum_fusion.2
  87.8 0.7 gather_fusion.2
  88.4 1.4 broadcast_select_fusion
  89.9 2.6 %collective-permute-done.4 = bf16[128,1024]{1,0:T(8,128)(2,1)} collective-permute-done((bf16[128,1024]{1,0:T(8,128)(2,1)S(1)}, bf16[128,1024]{1,0:T(8,128)(2,1)}, u32[]{:S(2)}, u32[]{:S(2)}) %collective-permute-start.4) | collective-permute-done | bytes 262176 | tf_op jit(solution)/shard_map/ppermute | solution.py:43
  92.5 0.7 copy-done.7
  93.2 1.2 pad_maximum_fusion
  94.4 0.7 gather_fusion.1
  95.1 14.3 %all-to-all-done.1 = bf16[32,32,3,512]{3,1,2,0:T(8,128)(2,1)} async-done(((bf16[32,32,3,512]{3,1,2,0:T(8,128)(2,1)}), bf16[32,32,3,512]{3,1,2,0:T(8,128)(2,1)}, u32[]{:S(2)}, u32[]{:S(2)}) %all-to-all-start.1) | async-done | bytes 3145760 | tf_op jit(solution)/shard_map/all_to_all | solution.py:110
  109.4 2.5 %convert_reduce_fusion = f32[2,32,3,512]{3,1,2,0:T(8,128)S(1)} fusion(bf16[16,2,32,3,512]{4,2,3,1,0:T(8,128)(2,1)} %bitcast.81), kind=kLoop, calls=%fused_computation.3 | loop fusion | flops 3047424 | bytes 3538944 | tf_op jit(solution)/shard_map/reduce_sum | solution.py:113
  114.3 3.5 %fusion.68 = (f32[2,16,4]{1,2,0:T(4,128)S(1)}, f32[2,16,4,1024]{3,1,2,0:T(8,128)S(1)}) fusion(bf16[2,128,4,8,256]{4,3,2,1,0:T(8,128)(2,1)} %bitcast.285, bf16[2,16,4,64]{3,1,2,0:T(8,128)(2,1)S(1)} %copy.238, pred[2,1024]{1,0:T(4,128)(4,1)S(1)} %copy-done.12, bf16[2,16,4,192]{3,1,0,2:T(8,128)(2,1)S(1)} %bitcast.329), kind=kOutput, calls=%fused_computation.206 | convolution fusion | flops 67633024 | bytes 4786688 | tf_op jit(solution)/shard_map/gqhd,gjhd->gqhj/dot_general | solution.py:131
  117.8 2.2 %fusion.9 = f32[32,4,1,32]{3,2,1,0:T(1,128)S(1)} fusion(bf16[32,4,4,8,256]{4,3,2,1,0:T(8,128)(2,1)} %bitcast.348, bf16[32,4,256,1]{2,0,1,3:T(8,128)(2,1)S(1)} %get-tuple-element.25), kind=kOutput, calls=%fused_computation.15 | convolution fusion | flops 2097152 | bytes 2179072 | tf_op jit(solution)/shard_map/rhd,rthd->rht/dot_general | solution.py:139
  120.3 6.5 %fusion.37 = bf16[1024,128]{1,0:T(8,128)(2,1)} fusion(bf16[1024,4096]{1,0:T(8,128)(2,1)} %all-gather.3.cloned.1.call-done, bf16[4096,128]{1,0:T(8,128)(2,1)S(1)} %copy-done, f32[128]{0:T(128)S(1)} %copy-done.19), kind=kOutput, calls=%fused_computation.47 | convolution fusion | flops 1075052544 | bytes 9699840 | tf_op jit(solution)/shard_map/dot_general | solution.py:193
  126.8 2.9 %fusion.21 = f32[2,16,4,256]{3,1,2,0:T(8,128)S(1)} fusion(bf16[2,128,4,8,256]{4,3,2,1,0:T(8,128)(2,1)} %bitcast.288, f32[2,16,4,1024]{3,1,2,0:T(8,128)S(1)} %get-tuple-element.32, f32[2,16,4]{1,2,0:T(4,128)S(1)} %copy.245), kind=kOutput, calls=%fused_computation.25 | convolution fusion | flops 67371008 | bytes 4850176 | tf_op jit(solution)/shard_map/gqhj,gjhd->gqhd/dot_general | solution.py:157
  130.2 2.0 %fusion.6 = f32[32,4,1,256]{3,2,1,0:T(1,128)S(1)} fusion(bf16[32,4,4,8,256]{4,3,2,1,0:T(8,128)(2,1)} %bitcast.349, bf16[32,4,32,1]{2,0,1,3:T(8,128)(2,1)S(1)} %get-tuple-element.28), kind=kOutput, calls=%fused_computation.12 | convolution fusion | flops 2097152 | bytes 2236416 | tf_op jit(solution)/shard_map/rht,rthd->rhd/dot_general | solution.py:164
  132.7 1.5 reshape.376
  134.3 7.2 %all-to-all-start.2 = ((bf16[128,2,512]{2,1,0:T(2,128)(2,1)}), bf16[128,2,512]{2,1,0:T(2,128)(2,1)S(1)}, u32[]{:S(2)}, u32[]{:S(2)}) async-start(bf16[128,2,512]{2,1,0:T(2,128)(2,1)} %reshape.376), calls=%async_computation.2 | async-start | bytes 524288 | tf_op jit(solution)/shard_map/all_to_all | solution.py:178
  141.7 12.9 %all-to-all-done.2 = bf16[128,2,512]{2,1,0:T(2,128)(2,1)S(1)} async-done(((bf16[128,2,512]{2,1,0:T(2,128)(2,1)}), bf16[128,2,512]{2,1,0:T(2,128)(2,1)S(1)}, u32[]{:S(2)}, u32[]{:S(2)}) %all-to-all-start.2) | async-done | bytes 262176 | tf_op jit(solution)/shard_map/all_to_all | solution.py:178
  155.8 1.1 reshape.329
  156.9 2.5 %fusion.69 = f32[1024,1024]{1,0:T(8,128)S(1)} fusion(bf16[1024,512]{1,0:T(8,128)(2,1)} %all-gather.5.cloned.1.call-done, bf16[512,1024]{1,0:T(8,128)(2,1)S(1)} %bitcast_select_fusion), kind=kOutput, calls=%fused_computation.207 | convolution fusion | flops 1073741824 | bytes 6291456 | tf_op jit(solution)/shard_map/dot_general | solution.py:197
  159.4 0.8 bitcast_add_fusion
  160.8 2.3 %collective-permute-done.10 = bf16[1024,512]{1,0:T(8,128)(2,1)S(1)} collective-permute-done((bf16[1024,512]{1,0:T(8,128)(2,1)S(1)}, bf16[1024,512]{1,0:T(8,128)(2,1)S(1)}, u32[]{:S(2)}, u32[]{:S(2)}) %collective-permute-start.10) | collective-permute-done | bytes 1048608 | tf_op jit(solution)/shard_map/ppermute | solution.py:203
  163.1 1.4 add_convert_fusion
  164.5 4.5 %all-to-all-start.3 = ((bf16[32,32,512]{2,1,0:T(8,128)(2,1)}), bf16[32,32,512]{2,1,0:T(8,128)(2,1)S(1)}, u32[]{:S(2)}, u32[]{:S(2)}) async-start(bf16[32,32,512]{2,1,0:T(8,128)(2,1)} %bitcast.77), calls=%async_computation.3 | async-start | bytes 2097152 | tf_op jit(solution)/shard_map/all_to_all | solution.py:205
  169.0 17.0 %all-to-all-done.3 = bf16[32,32,512]{2,1,0:T(8,128)(2,1)S(1)} async-done(((bf16[32,32,512]{2,1,0:T(8,128)(2,1)}), bf16[32,32,512]{2,1,0:T(8,128)(2,1)S(1)}, u32[]{:S(2)}, u32[]{:S(2)}) %all-to-all-start.3) | async-done | bytes 1048608 | tf_op jit(solution)/shard_map/all_to_all | solution.py:205
  (169 shorter events, 32.5 us)
Async XLA Ops:
  6.5 113.8 %copy-start = (bf16[4096,128]{1,0:T(8,128)(2,1)S(1)}, bf16[4096,128]{1,0:T(8,128)(2,1)}, u32[]{:S(2)}) copy-start(bf16[4096,128]{1,0:T(8,128)(2,1)} %param.26) | copy-start | bytes 3145732
  6.5 11.4 %copy-start.10 = (bf16[4096]{0:T(1024)(128)(2,1)S(1)}, bf16[4096]{0:T(1024)(128)(2,1)}, u32[]{:S(2)}) copy-start(bf16[4096]{0:T(1024)(128)(2,1)} %param.16) | copy-start | bytes 24580
  6.5 11.4 %copy-start.11 = (bf16[4096]{0:T(1024)(128)(2,1)S(1)}, bf16[4096]{0:T(1024)(128)(2,1)}, u32[]{:S(2)}) copy-start(bf16[4096]{0:T(1024)(128)(2,1)} %param.17) | copy-start | bytes 24580
  6.5 113.8 %all-gather.3.cloned.1.call-start = ((), (), s32[]{:S(2)}) async-start(), calls=%async_computation.4 | async-start | bytes 8650752 | tf_op jit(solution)/shard_map/all_gather | solution.py:85
  6.5 6.6 %collective-permute-start = (bf16[32,1024]{1,0:T(8,128)(2,1)}, bf16[32,1024]{1,0:T(8,128)(2,1)S(1)}, u32[]{:S(2)}, u32[]{:S(2)}) collective-permute-start(bf16[32,1024]{1,0:T(8,128)(2,1)} %param.15), channel_id=1, source_target_pairs={{0,1},{1,2},{2,3},{3,0},{4,5},{5,6},{6,7},{7,4},{8,9},{9,10},{10,1... | collective-permute-start | bytes 196616 | tf_op jit(solution)/shard_map/ppermute | solution.py:55
  8.6 4.5 %collective-permute-start.2 = (bf16[32,1024]{1,0:T(8,128)(2,1)}, bf16[32,1024]{1,0:T(8,128)(2,1)S(1)}, u32[]{:S(2)}, u32[]{:S(2)}) collective-permute-start(bf16[32,1024]{1,0:T(8,128)(2,1)} %param.15), channel_id=1, source_target_pairs={{0,3},{1,0},{2,1},{3,2},{4,7},{5,4},{6,5},{7,6},{8,11},{9,8},{10,9... | collective-permute-start | bytes 196616 | tf_op jit(solution)/shard_map/ppermute | solution.py:55
  10.0 4.8 %collective-permute-start.1 = (bf16[32,1024]{1,0:T(8,128)(2,1)}, bf16[32,1024]{1,0:T(8,128)(2,1)S(1)}, u32[]{:S(2)}, u32[]{:S(2)}) collective-permute-start(bf16[32,1024]{1,0:T(8,128)(2,1)} %param.15), channel_id=1, source_target_pairs={{0,2},{1,3},{2,0},{3,1},{4,6},{5,7},{6,4},{7,5},{8,10},{9,11},{10,... | collective-permute-start | bytes 196616 | tf_op jit(solution)/shard_map/ppermute | solution.py:55
  11.7 4.6 %copy-start.14 = (s32[1024]{0:T(1024)}, s32[1024]{0:T(1024)S(1)}, u32[]{:S(2)}) copy-start(s32[1024]{0:T(1024)S(1)} %pad_clamp_fusion) | copy-start | bytes 12292
  13.1 4.9 %copy-start.13 = (pred[4]{0:T(512)(128)(4,1)}, pred[4]{0:T(512)(128)(4,1)S(1)}, u32[]{:S(2)}) copy-start(pred[4]{0:T(512)(128)(4,1)S(1)} %compare_and_fusion) | copy-start | bytes 16
  18.0 30.8 %copy-start.3 = (bf16[128,3,1024]{2,0,1:T(8,128)(2,1)S(1)}, bf16[128,3,1024]{2,0,1:T(8,128)(2,1)}, u32[]{:S(2)}) copy-start(bf16[128,3,1024]{2,0,1:T(8,128)(2,1)} %param.18) | copy-start | bytes 2359300
  38.2 24.3 %all-to-all-start = ((bf16[32,32,1,256]{3,1,2,0:T(8,128)(2,1)}), bf16[32,32,1,256]{3,1,2,0:T(8,128)(2,1)S(1)}, u32[]{:S(2)}, u32[]{:S(2)}) async-start(bf16[32,32,1,256]{3,1,2,0:T(8,128)(2,1)} %constant_dynamic-update-slice_fusion), calls=%async_computation | async-start | bytes 1048576 | tf_op jit(solution)/shard_map/all_to_all | solution.py:89
  48.9 1.8 collective-permute-start.6
  65.6 5.3 %copy-start.5 = (bf16[8,4,4096]{2,1,0:T(4,128)(2,1)S(1)}, bf16[8,4,4096]{2,1,0:T(4,128)(2,1)}, u32[]{:S(2)}) copy-start(bf16[8,4,4096]{2,1,0:T(4,128)(2,1)} %param.25) | copy-start | bytes 786436
  65.6 10.1 %copy-start.2 = (bf16[128,4096]{1,0:T(8,128)(2,1)S(1)}, bf16[128,4096]{1,0:T(8,128)(2,1)}, u32[]{:S(2)}) copy-start(bf16[128,4096]{1,0:T(8,128)(2,1)} %param.28) | copy-start | bytes 3145732
  65.6 43.7 %all-to-all-start.1 = ((bf16[32,32,3,512]{3,1,2,0:T(8,128)(2,1)}), bf16[32,32,3,512]{3,1,2,0:T(8,128)(2,1)}, u32[]{:S(2)}, u32[]{:S(2)}) async-start(bf16[32,32,3,512]{3,1,2,0:T(8,128)(2,1)} %copy.233), calls=%async_computation.1 | async-start | bytes 6291456 | tf_op jit(solution)/shard_map/all_to_all | solution.py:110
  70.8 86.1 %all-gather.5.cloned.1.call-start = ((), (), s32[]{:S(2)}) async-start(), calls=%async_computation.5 | async-start | bytes 1310720 | tf_op jit(solution)/shard_map/all_gather | solution.py:196
  71.8 8.4 %copy-start.18 = (s32[2]{0:T(128)S(1)}, s32[2]{0:T(128)}, u32[]{:S(2)}) copy-start(s32[2]{0:T(128)} %param.23) | copy-start | bytes 28
  71.8 8.5 %copy-start.17 = (s32[32]{0:T(128)S(1)}, s32[32]{0:T(128)}, u32[]{:S(2)}) copy-start(s32[32]{0:T(128)} %param.24) | copy-start | bytes 388
  72.5 12.6 %collective-permute-start.9 = (bf16[8,4,1024]{2,0,1:T(8,128)(2,1)}, bf16[8,4,1024]{2,0,1:T(8,128)(2,1)}, u32[]{:S(2)}, u32[]{:S(2)}) collective-permute-start(bf16[8,4,1024]{2,0,1:T(8,128)(2,1)} %bitcast.280), channel_id=1, source_target_pairs={{0,3},{1,0},{2,1},{3,2},{4,7},{5,4},{6,5},{7,6},{8,11},{9,8},{10,9... | collective-permute-start | bytes 196616 | tf_op jit(solution)/shard_map/ppermute | solution.py:43
  73.3 13.5 %collective-permute-start.7 = (bf16[8,4,1024]{2,0,1:T(8,128)(2,1)}, bf16[8,4,1024]{2,0,1:T(8,128)(2,1)}, u32[]{:S(2)}, u32[]{:S(2)}) collective-permute-start(bf16[8,4,1024]{2,0,1:T(8,128)(2,1)} %bitcast.282), channel_id=1, source_target_pairs={{0,1},{1,2},{2,3},{3,0},{4,5},{5,6},{6,7},{7,4},{8,9},{9,10},{10,1... | collective-permute-start | bytes 196616 | tf_op jit(solution)/shard_map/ppermute | solution.py:43
  75.4 11.4 %collective-permute-start.8 = (bf16[8,4,1024]{2,0,1:T(8,128)(2,1)}, bf16[8,4,1024]{2,0,1:T(8,128)(2,1)}, u32[]{:S(2)}, u32[]{:S(2)}) collective-permute-start(bf16[8,4,1024]{2,0,1:T(8,128)(2,1)} %bitcast.281), channel_id=1, source_target_pairs={{0,2},{1,3},{2,0},{3,1},{4,6},{5,7},{6,4},{7,5},{8,10},{9,11},{10,... | collective-permute-start | bytes 196616 | tf_op jit(solution)/shard_map/ppermute | solution.py:43
  76.6 13.2 %collective-permute-start.3 = (bf16[128,1024]{1,0:T(8,128)(2,1)S(1)}, bf16[128,1024]{1,0:T(8,128)(2,1)S(1)}, u32[]{:S(2)}, u32[]{:S(2)}) collective-permute-start(bf16[128,1024]{1,0:T(8,128)(2,1)S(1)} %bitcast.338), channel_id=1, source_target_pairs={{0,1},{1,2},{2,3},{3,0},{4,5},{5,6},{6,7},{7,4},{8,9},{9,10},{10,1... | collective-permute-start | bytes 786440 | tf_op jit(solution)/shard_map/ppermute | solution.py:43
  78.4 14.1 %collective-permute-start.4 = (bf16[128,1024]{1,0:T(8,128)(2,1)S(1)}, bf16[128,1024]{1,0:T(8,128)(2,1)}, u32[]{:S(2)}, u32[]{:S(2)}) collective-permute-start(bf16[128,1024]{1,0:T(8,128)(2,1)S(1)} %bitcast.339), channel_id=1, source_target_pairs={{0,2},{1,3},{2,0},{3,1},{4,6},{5,7},{6,4},{7,5},{8,10},{9,11},{10,... | collective-permute-start | bytes 786440 | tf_op jit(solution)/shard_map/ppermute | solution.py:43
  85.1 7.4 %collective-permute-start.5 = (bf16[128,1024]{1,0:T(8,128)(2,1)S(1)}, bf16[128,1024]{1,0:T(8,128)(2,1)S(1)}, u32[]{:S(2)}, u32[]{:S(2)}) collective-permute-start(bf16[128,1024]{1,0:T(8,128)(2,1)S(1)} %bitcast.340), channel_id=1, source_target_pairs={{0,3},{1,0},{2,1},{3,2},{4,7},{5,4},{6,5},{7,6},{8,11},{9,8},{10,9... | collective-permute-start | bytes 786440 | tf_op jit(solution)/shard_map/ppermute | solution.py:43
  92.5 0.7 copy-start.7
  109.4 3.2 %copy-start.8 = (f32[32,32]{0,1:T(8,128)S(1)}, f32[32,32]{0,1:T(8,128)}, u32[]{:S(2)}) copy-start(f32[32,32]{0,1:T(8,128)} %get-tuple-element.30) | copy-start | bytes 12292
  111.9 2.4 %copy-start.12 = (pred[2,1024]{1,0:T(4,128)(4,1)S(1)}, pred[2,1024]{1,0:T(4,128)(4,1)}, u32[]{:S(2)}) copy-start(pred[2,1024]{1,0:T(4,128)(4,1)} %iota_compare_fusion.1) | copy-start | bytes 6148
  114.3 5.8 %copy-start.9 = (pred[32,32]{1,0:T(8,128)(4,1)S(1)}, pred[32,32]{1,0:T(8,128)(4,1)}, u32[]{:S(2)}) copy-start(pred[32,32]{1,0:T(8,128)(4,1)} %iota_compare_fusion) | copy-start | bytes 3076
  114.3 6.0 %copy-start.19 = (f32[128]{0:T(128)S(1)}, f32[128]{0:T(128)}, u32[]{:S(2)}) copy-start(f32[128]{0:T(128)} %convert_element_type.110) | copy-start | bytes 1540
  130.2 11.2 %copy-start.16 = (pred[512]{0:T(512)(128)(4,1)S(1)}, pred[512]{0:T(512)(128)(4,1)}, u32[]{:S(2)}) copy-start(pred[512]{0:T(512)(128)(4,1)} %broadcast_bitcast_fusion) | copy-start | bytes 1540
  134.3 20.3 %all-to-all-start.2 = ((bf16[128,2,512]{2,1,0:T(2,128)(2,1)}), bf16[128,2,512]{2,1,0:T(2,128)(2,1)S(1)}, u32[]{:S(2)}, u32[]{:S(2)}) async-start(bf16[128,2,512]{2,1,0:T(2,128)(2,1)} %reshape.376), calls=%async_computation.2 | async-start | bytes 524288 | tf_op jit(solution)/shard_map/all_to_all | solution.py:178
  156.8 2.6 %copy-start.4 = (bf16[4,8,4,1024]{3,1,2,0:T(8,128)(2,1)S(1)}, bf16[4,8,4,1024]{3,1,2,0:T(8,128)(2,1)}, u32[]{:S(2)}) copy-start(bf16[4,8,4,1024]{3,1,2,0:T(8,128)(2,1)} %broadcast_select_fusion) | copy-start | bytes 786436
  160.2 26.7 %copy-start.1 = (bf16[4096,128]{1,0:T(8,128)(2,1)S(1)}, bf16[4096,128]{1,0:T(8,128)(2,1)}, u32[]{:S(2)}) copy-start(bf16[4096,128]{1,0:T(8,128)(2,1)} %param.26) | copy-start | bytes 3145732
  160.4 8.6 %copy-start.15 = (bf16[1024]{0:T(1024)(128)(2,1)S(1)}, bf16[1024]{0:T(1024)(128)(2,1)}, u32[]{:S(2)}) copy-start(bf16[1024]{0:T(1024)(128)(2,1)} %param.29) | copy-start | bytes 6148
  160.4 25.8 %copy-start.6 = (bf16[32,1024]{1,0:T(8,128)(2,1)S(1)}, bf16[32,1024]{1,0:T(8,128)(2,1)}, u32[]{:S(2)}) copy-start(bf16[32,1024]{1,0:T(8,128)(2,1)} %param.15) | copy-start | bytes 196612
  160.4 2.7 %collective-permute-start.10 = (bf16[1024,512]{1,0:T(8,128)(2,1)S(1)}, bf16[1024,512]{1,0:T(8,128)(2,1)S(1)}, u32[]{:S(2)}, u32[]{:S(2)}) collective-permute-start(bf16[1024,512]{1,0:T(8,128)(2,1)S(1)} %dynamic-slice_convert_fusion), channel_id=1, source_target_pairs={{0,4},{4,0},{8,12},{12,8},{16,20},{20,16},{24,28},{28,24},{32,36},... | collective-permute-start | bytes 3145736 | tf_op jit(solution)/shard_map/ppermute | solution.py:203
  164.5 21.5 %all-to-all-start.3 = ((bf16[32,32,512]{2,1,0:T(8,128)(2,1)}), bf16[32,32,512]{2,1,0:T(8,128)(2,1)S(1)}, u32[]{:S(2)}, u32[]{:S(2)}) async-start(bf16[32,32,512]{2,1,0:T(8,128)(2,1)} %bitcast.77), calls=%async_computation.3 | async-start | bytes 2097152 | tf_op jit(solution)/shard_map/all_to_all | solution.py:205
Sparse Core Ops, SparseCore 0:
  18.0 62.6 all-gather.2
  126.9 24.6 all-gather.4
